TPU v7x, 32 devices: a whole 2x2x4 slice. The times are simulated.
32 devices in a mesh: row: 8 (over y, x, core), col: 4 (over z).
Axes of the slice: x: 2, y: 2, z: 4, core: 2. Of those that a mesh axis runs over, the one named last changes fastest.
Arguments:
- tokens: bfloat16 [192, 8192], P('col', 'row'), may hold values from -6 to 6
- grad_out: bfloat16 [192, 8192], P('col', 'row'), may hold values from -6 to 6
- gate_weight: bfloat16 [8192, 14336], P('row', 'col'), may hold values from -0.0625 to 0.0625
- up_weight: bfloat16 [8192, 14336], P('row', 'col'), may hold values from -0.0625 to 0.0625
- down_weight: bfloat16 [14336, 8192], P('col', 'row'), may hold values from -0.046875 to 0.046875
Outputs:
- grad_tokens: bfloat16 [192, 8192], P('col', 'row')
- grad_gate_weight: bfloat16 [8192, 14336], P('row', 'col')
- grad_up_weight: bfloat16 [8192, 14336], P('row', 'col')
- grad_down_weight: bfloat16 [14336, 8192], P('col', 'row')
All inputs are finite; a program needn't handle non-finite values.
Results may differ from a plain program's by a relative error of at most 0.024.
Values may be sent and summed in bfloat16 or wider, within the bound.
No kernel may reach another device: no remote copies, remote signals or barrier semaphores. Data moves between devices by JAX's collectives and lax.ppermute only.
A program may use at most 128 MiB of HBM per device.

v0:
```python
import jax
import jax.numpy as jnp
from jax import lax
from jax.sharding import PartitionSpec as P


def contract_first(left, right):
    return lax.dot_general(
        left, right, (((0,), (0,)), ((), ())), preferred_element_type=jnp.float32
    )


def contract_last(left, right):
    return lax.dot_general(
        left, right, (((1,), (1,)), ((), ())), preferred_element_type=jnp.float32
    )


def gated_grads(gate_sum, up_sum, grad_hidden):
    sigmoid_gate = jax.nn.sigmoid(gate_sum)
    hidden = (gate_sum * sigmoid_gate * up_sum).astype(jnp.bfloat16)
    grad_up = (grad_hidden * gate_sum * sigmoid_gate).astype(jnp.bfloat16)
    grad_gate = (
        grad_hidden * up_sum * sigmoid_gate * (1.0 + gate_sum * (1.0 - sigmoid_gate))
    ).astype(jnp.bfloat16)
    return (hidden, grad_gate, grad_up)


def body(tokens, grad_out, gate_weight, up_weight, down_weight):
    tok_all, grad_all = (
        lax.all_gather(tokens, "col", axis=0, tiled=True),
        lax.all_gather(grad_out, "col", axis=0, tiled=True),
    )
    gate_sum, up_sum, grad_hidden = (
        lax.psum(
            jnp.dot(tok_all, gate_weight, preferred_element_type=jnp.float32).astype(jnp.bfloat16),
            "row",
        ).astype(jnp.float32),
        lax.psum(
            jnp.dot(tok_all, up_weight, preferred_element_type=jnp.float32).astype(jnp.bfloat16),
            "row",
        ).astype(jnp.float32),
        lax.psum(contract_last(grad_all, down_weight).astype(jnp.bfloat16), "row").astype(
            jnp.float32
        ),
    )
    hidden, grad_gate, grad_up = gated_grads(gate_sum, up_sum, grad_hidden)
    acc_gate = contract_first(tok_all, grad_gate)
    acc_up = contract_first(tok_all, grad_up)
    acc_down = contract_first(hidden, grad_all)
    partial_grad = contract_last(grad_gate, gate_weight) + contract_last(grad_up, up_weight)
    grad_tokens = lax.psum_scatter(
        partial_grad.astype(jnp.bfloat16), "col", scatter_dimension=0, tiled=True
    )
    return (
        grad_tokens,
        acc_gate.astype(jnp.bfloat16),
        acc_up.astype(jnp.bfloat16),
        acc_down.astype(jnp.bfloat16),
    )


def solution(mesh):
    return jax.shard_map(
        body,
        mesh=mesh,
        in_specs=(
            P("col", "row"),
            P("col", "row"),
            P("row", "col"),
            P("row", "col"),
            P("col", "row"),
        ),
        out_specs=(P("col", "row"), P("row", "col"), P("row", "col"), P("col", "row")),
        check_vma=False,
    )
```

profile of v0, /device:TPU:0, one launch (start us, length us, event | category | flops | bytes accessed | tf_op | source)
XLA Modules:
  0.0 188.0 jit_solution(11670191383653160460)
XLA Ops:
  7.2 0.0 all-reduce.3.cloned.1.call-start
  7.2 16.5 %all_gather.7 = bf16[192,1024]{1,0:T(8,128)(2,1)S(1)} all-gather(bf16[48,1024]{1,0:T(8,128)(2,1)} %param.5), channel_id=1, replica_groups=mesh['row'=8,'col'=4] {'col'}, dimensions={0}, use_global_device_ids=true | all-gather | bytes 491520 | tf_op jit(solution)/shard_map/all_gather | solution.py:31
  23.7 15.8 %all_gather.6 = bf16[192,1024]{1,0:T(8,128)(2,1)S(1)} all-gather(bf16[48,1024]{1,0:T(8,128)(2,1)} %param.6), channel_id=1, replica_groups=mesh['row'=8,'col'=4] {'col'}, dimensions={0}, use_global_device_ids=true | all-gather | bytes 491520 | tf_op jit(solution)/shard_map/all_gather | solution.py:32
  39.4 0.0 copy-start.4
  39.4 0.0 slice-start
  39.4 5.9 %convolution_convert_fusion.4 = bf16[192,3584]{1,0:T(8,128)(2,1)} fusion(bf16[192,1024]{1,0:T(8,128)(2,1)S(1)} %all_gather.7, bf16[1024,3584]{1,0:T(8,128)(2,1)} %param.8), kind=kOutput, calls=%fused_computation.6 | convolution fusion | flops 1409974272 | bytes 9109504 | tf_op jit(solution)/shard_map/dot_general | solution.py:40
  45.4 0.0 copy-done.4
  45.4 0.0 slice-start.1
  45.4 2.7 %convolution_convert_fusion.3 = bf16[192,3584]{1,0:T(8,128)(2,1)} fusion(bf16[192,1024]{1,0:T(8,128)(2,1)S(1)} %all_gather.7, bf16[1024,3584]{1,0:T(8,128)(2,1)S(1)} %copy-done.4), kind=kOutput, calls=%fused_computation.5 | convolution fusion | flops 1409974272 | bytes 9109504 | tf_op jit(solution)/shard_map/dot_general | solution.py:36
  48.1 0.0 slice-done
  48.1 0.0 slice-done.1
  48.1 3.6 %convolution_convert_fusion.5 = bf16[192,3584]{1,0:T(8,128)(2,1)} fusion(bf16[192,1024]{1,0:T(8,128)(2,1)S(1)} %all_gather.6, bf16[3584,1024]{1,0:T(8,128)(2,1)S(1)} %bitcast.18), kind=kOutput, calls=%fused_computation.7 | convolution fusion | flops 1409974272 | bytes 9109504 | tf_op jit(solution)/shard_map/dot_general | solution.py:14
  51.7 0.0 all-reduce.3.cloned.1.call-update
  51.7 0.2 reduce-scatter.2.cloned.1.call-start
  51.9 81.2 %all-reduce.3.cloned.1.call-done = (bf16[192,3584]{1,0:T(8,128)(2,1)}, bf16[192,3584]{1,0:T(8,128)(2,1)}, bf16[192,3584]{1,0:T(8,128)(2,1)}) async-done(((bf16[192,3584]{1,0:T(8,128)(2,1)}, bf16[192,3584]{1,0:T(8,128)(2,1)}, bf16[192,3584]{1,0:T(8,128)(2,1)}), (bf16[192,3584]{1,0:T(8,128)(2,1)}, bf16[192,3584]{1,0:T(8,128)(2,1)}, bf16[192,3584]{1,0:T(8,128)(2,1)})) %all-reduce.3.cloned.1.call-update) | async-done | bytes 4128784 | tf_op jit(solution)/shard_map/psum | solution.py:39
  133.2 0.0 copy-start
  133.2 0.0 copy-start.1
  133.2 0.0 copy-start.3
  133.2 7.0 %fusion.1 = bf16[1024,3584]{0,1:T(8,128)(2,1)} fusion(bf16[192,1024]{1,0:T(8,128)(2,1)S(1)} %all_gather.7, bf16[192,3584]{1,0:T(8,128)(2,1)} %get-tuple-element.10, bf16[192,3584]{1,0:T(8,128)(2,1)} %get-tuple-element.9), kind=kOutput, calls=%fused_computation.4 | convolution fusion | flops 1418461184 | bytes 10485760 | tf_op jit(solution)/shard_map/dot_general | solution.py:8
  140.2 0.0 copy-done
  140.2 0.0 copy-done.1
  140.2 0.0 copy-done.3
  140.2 0.0 slice-start.2
  140.3 1.2 fusion.4
  141.5 0.0 slice-start.3
  141.5 5.7 %fusion.18 = f32[192,1024]{1,0:T(8,128)S(1)} fusion(bf16[192,3584]{1,0:T(8,128)(2,1)S(1)} %fusion.4, bf16[1024,3584]{1,0:T(8,128)(2,1)} %param.7), kind=kOutput, calls=%fused_computation.28 | convolution fusion | flops 1409286144 | bytes 9502720 | tf_op jit(solution)/shard_map/dot_general | solution.py:14
  147.2 0.0 slice-done.2
  147.3 0.0 slice-done.3
  147.3 3.4 %fusion.14 = bf16[192,1024]{1,0:T(8,128)(2,1)} fusion(f32[192,1024]{1,0:T(8,128)S(1)} %fusion.18, bf16[1024,3584]{1,0:T(8,128)(2,1)S(1)} %bitcast.20, bf16[192,3584]{1,0:T(8,128)(2,1)S(1)} %copy-done.1, bf16[192,3584]{1,0:T(8,128)(2,1)S(1)} %copy-done.3), kind=kOutput, calls=%fused_computation.26 | convolution fusion | flops 1415184384 | bytes 11272192 | tf_op jit(solution)/shard_map/dot_general | solution.py:14
  150.6 0.0 reduce-scatter.2.cloned.1.call-update
  150.7 5.2 %fusion = bf16[1024,3584]{0,1:T(8,128)(2,1)} fusion(bf16[192,3584]{1,0:T(8,128)(2,1)S(1)} %fusion.4, bf16[192,1024]{1,0:T(8,128)(2,1)S(1)} %all_gather.7), kind=kOutput, calls=%fused_computation.3 | convolution fusion | flops 1412956160 | bytes 9109504 | tf_op jit(solution)/shard_map/dot_general | solution.py:8
  155.8 10.0 %copy.9 = bf16[1024,3584]{1,0:T(8,128)(2,1)} copy(bf16[1024,3584]{0,1:T(8,128)(2,1)} %fusion) | data formatting | bytes 14680064
  165.8 0.0 copy-start.2
  165.8 10.0 %copy.10 = bf16[1024,3584]{1,0:T(8,128)(2,1)} copy(bf16[1024,3584]{0,1:T(8,128)(2,1)} %fusion.1) | data formatting | bytes 14680064
  175.8 0.0 copy-done.2
  175.8 5.3 %convolution_convert_fusion = bf16[3584,1024]{1,0:T(8,128)(2,1)} fusion(bf16[192,1024]{1,0:T(8,128)(2,1)S(1)} %all_gather.6, bf16[192,3584]{1,0:T(8,128)(2,1)S(1)} %copy-done, bf16[192,3584]{1,0:T(8,128)(2,1)S(1)} %copy-done.2), kind=kOutput, calls=%fused_computation | convolution fusion | flops 1418461184 | bytes 10485760 | tf_op jit(solution)/shard_map/dot_general | solution.py:8
  181.1 0.0 reduce-scatter.2.cloned.1.call-done
  (2 shorter events, 0.0 us)
Async XLA Ops:
  7.2 126.0 %all-reduce.3.cloned.1.call-start = ((), (), s32[]{:S(2)}) async-start(), calls=%async_computation.2 | async-start | bytes 8257536 | tf_op jit(solution)/shard_map/psum | solution.py:39
  39.4 5.9 %copy-start.4 = (bf16[1024,3584]{1,0:T(8,128)(2,1)S(1)}, bf16[1024,3584]{1,0:T(8,128)(2,1)}, u32[]{:S(2)}) copy-start(bf16[1024,3584]{1,0:T(8,128)(2,1)} %param.7) | copy-start | bytes 22020100
  39.4 8.6 %slice-start = ((s8[7340032]{0:T(1024)(128)(4,1)}), s8[4194304]{0:T(1024)(128)(4,1)S(1)}, s32[]{:S(2)}) async-start(s8[7340032]{0:T(1024)(128)(4,1)} %bitcast.17), calls=%async_computation.3 | async-start | bytes 8388608
  45.4 2.7 %slice-start.1 = ((s8[7340032]{0:T(1024)(128)(4,1)}), s8[3145728]{0:T(1024)(128)(4,1)S(1)}, s32[]{:S(2)}) async-start(s8[7340032]{0:T(1024)(128)(4,1)} %bitcast.17), calls=%async_computation.4 | async-start | bytes 6291456
  51.7 129.4 %reduce-scatter.2.cloned.1.call-start = ((), (), s32[]{:S(2)}) async-start(), calls=%async_computation.1 | async-start | bytes 491520 | tf_op jit(solution)/shard_map/reduce_scatter | solution.py:52
  133.2 7.1 %copy-start = (bf16[192,3584]{1,0:T(8,128)(2,1)S(1)}, bf16[192,3584]{1,0:T(8,128)(2,1)}, u32[]{:S(2)}) copy-start(bf16[192,3584]{1,0:T(8,128)(2,1)} %get-tuple-element.8) | copy-start | bytes 4128772
  133.2 7.1 %copy-start.1 = (bf16[192,3584]{1,0:T(8,128)(2,1)S(1)}, bf16[192,3584]{1,0:T(8,128)(2,1)}, u32[]{:S(2)}) copy-start(bf16[192,3584]{1,0:T(8,128)(2,1)} %get-tuple-element.10) | copy-start | bytes 4128772
  133.2 7.1 %copy-start.3 = (bf16[192,3584]{1,0:T(8,128)(2,1)S(1)}, bf16[192,3584]{1,0:T(8,128)(2,1)}, u32[]{:S(2)}) copy-start(bf16[192,3584]{1,0:T(8,128)(2,1)} %get-tuple-element.9) | copy-start | bytes 4128772
  140.2 7.0 %slice-start.2 = ((s8[7340032]{0:T(1024)(128)(4,1)}), s8[4194304]{0:T(1024)(128)(4,1)S(1)}, s32[]{:S(2)}) async-start(s8[7340032]{0:T(1024)(128)(4,1)} %bitcast.19), calls=%async_computation.5 | async-start | bytes 8388608
  141.5 5.8 %slice-start.3 = ((s8[7340032]{0:T(1024)(128)(4,1)}), s8[3145728]{0:T(1024)(128)(4,1)S(1)}, s32[]{:S(2)}) async-start(s8[7340032]{0:T(1024)(128)(4,1)} %bitcast.19), calls=%async_computation.6 | async-start | bytes 6291456
  165.8 10.0 %copy-start.2 = (bf16[192,3584]{1,0:T(8,128)(2,1)S(1)}, bf16[192,3584]{1,0:T(8,128)(2,1)}, u32[]{:S(2)}) copy-start(bf16[192,3584]{1,0:T(8,128)(2,1)} %get-tuple-element.10) | copy-start | bytes 4128772
Sparse Core Ops, SparseCore 0:
  51.8 81.3 all-reduce.2
  150.8 20.8 reduce-scatter.1
where the time goes:
time: 189 us; the launch traced here: 188 us
  waiting for transfers between devices  81.3 us (43%)
  matrix products  38.8 us (21%)
  blocking collectives  32.2 us (17%)
  local copies, waits for them, and re-layouts  20.1 us (11%)
  between operations  14.1 us (7%)
    psum x1, waiting for transfers between devices, body(): lax.psum(jnp.dot(tok_all, up_weight, preferred_element_type=jnp.float32)....  81.2 us
    unnamed x20, local copies, waits for them, and re-layouts  20.1 us
    dot_general x3, matrix products, contract_first(): lax.dot_general(left, right, (((0,), (0,)), ((), ())), preferred_element_...  17.5 us
    all_gather x1, blocking collectives, body(): lax.all_gather(tokens, 'col', axis=0, tiled=True)  16.5 us
    all_gather x1, blocking collectives, body(): lax.all_gather(grad_out, 'col', axis=0, tiled=True)  15.8 us
    dot_general x3, matrix products, contract_last(): lax.dot_general(left, right, (((1,), (1,)), ((), ())), preferred_element_...  12.7 us
    dot_general x1, matrix products, body(): jnp.dot(tok_all, up_weight, preferred_element_type=jnp.float32)  5.91 us
  transfers between devices with their start and end apart: 2, of which 1 were waited for; matrix products, arithmetic and copies ran while one was open for 16% of the time, Pallas kernels for 0%

commit v1 on v0

--- a/solution.py
+++ b/solution.py
@@ -1,7 +1,15 @@
+import functools
 import jax
 import jax.numpy as jnp
 from jax import lax
 from jax.sharding import PartitionSpec as P
+
+
+def take_numbers(own_rows, mesh_name):
+    return jnp.sum(lax.all_gather(own_rows, mesh_name), axis=0)
+
+
+cover_pieces_all = functools.partial(take_numbers, mesh_name="row")
 
 
 def contract_first(left, right):
@@ -36,9 +44,8 @@
             jnp.dot(tok_all, gate_weight, preferred_element_type=jnp.float32).astype(jnp.bfloat16),
             "row",
         ).astype(jnp.float32),
-        lax.psum(
-            jnp.dot(tok_all, up_weight, preferred_element_type=jnp.float32).astype(jnp.bfloat16),
-            "row",
+        cover_pieces_all(
+            jnp.dot(tok_all, up_weight, preferred_element_type=jnp.float32).astype(jnp.bfloat16)
         ).astype(jnp.float32),
         lax.psum(contract_last(grad_all, down_weight).astype(jnp.bfloat16), "row").astype(
             jnp.float32

time: 189 us -> 233 us (1.23)
  waiting for transfers between devices: 81.3 us -> 112 us
  other arithmetic: 1.21 us -> 9.37 us
  matrix products: 38.8 us -> 44.9 us
    all_gather x0 -> x1, waiting for transfers between devices: none -> 50.4 us  [take_numbers(): return jnp.sum(lax.all_gather(own_rows, mesh_name), axis=0)]
    psum x1, waiting for transfers between devices: 81.2 us -> 60.9 us  [body(): lax.psum(contract_last(grad_all, down_weight).astype(jnp.bfloat16), 'row')]
    reduce_sum x0 -> x1, other arithmetic: none -> 6.42 us  [take_numbers(): return jnp.sum(lax.all_gather(own_rows, mesh_name), axis=0)]
    dot_general x1, matrix products: 2.7 us -> 5.91 us  [body(): jnp.dot(tok_all, gate_weight, preferred_element_type=jnp.float32)]
    dot_general x3, matrix products: 12.7 us -> 15.8 us  [contract_last(): lax.dot_general(left, right, (((1,), (1,)), ((), ())), preferred_element_...]
    unnamed x20 -> x12, local copies, waits for them, and re-layouts: 20.1 us -> 20.3 us
  transfers between devices with their start and end apart: 2 -> 3, of which waited for: 1 -> 3; matrix products, arithmetic and copies ran while one was open for 16% -> 19% of each run, Pallas kernels for 0% -> 0%
where the time goes in v1:
time: 233 us
  waiting for transfers between devices  112 us (48%)
  matrix products  44.9 us (19%)
  blocking collectives  32.4 us (14%)
  local copies, waits for them, and re-layouts  20.3 us (9%)
  between operations  13.8 us (6%)
  other arithmetic  9.37 us (4%)
    psum x1, waiting for transfers between devices, body(): lax.psum(contract_last(grad_all, down_weight).astype(jnp.bfloat16), 'row')  60.9 us
    all_gather x1, waiting for transfers between devices, take_numbers(): return jnp.sum(lax.all_gather(own_rows, mesh_name), axis=0)  50.4 us
    unnamed x12, local copies, waits for them, and re-layouts  20.3 us
    dot_general x3, matrix products, contract_first(): lax.dot_general(left, right, (((0,), (0,)), ((), ())), preferred_element_...  17.5 us
    all_gather x1, blocking collectives, body(): lax.all_gather(tokens, 'col', axis=0, tiled=True)  16.5 us
    all_gather x1, blocking collectives, body(): lax.all_gather(grad_out, 'col', axis=0, tiled=True)  15.9 us
    dot_general x3, matrix products, contract_last(): lax.dot_general(left, right, (((1,), (1,)), ((), ())), preferred_element_...  15.8 us
    reduce_sum x1, other arithmetic, take_numbers(): return jnp.sum(lax.all_gather(own_rows, mesh_name), axis=0)  6.42 us
  transfers between devices with their start and end apart: 3, of which 3 were waited for; matrix products, arithmetic and copies ran while one was open for 19% of the time, Pallas kernels for 0%

profile of v1, /device:TPU:0, one launch (start us, length us, event | category | flops | bytes accessed | tf_op | source)
XLA Modules:
  0.0 232.7 jit_solution(14774838372785459877)
XLA Ops:
  7.2 0.0 all-reduce.3.cloned.1.call-start
  7.2 16.5 %all_gather.13 = bf16[192,1024]{1,0:T(8,128)(2,1)S(1)} all-gather(bf16[48,1024]{1,0:T(8,128)(2,1)} %param.5), channel_id=1, replica_groups=mesh['row'=8,'col'=4] {'col'}, dimensions={0}, use_global_device_ids=true | all-gather | bytes 491520 | tf_op jit(solution)/shard_map/all_gather | solution.py:39
  23.7 0.0 slice-start
  23.7 15.9 %all_gather.12 = bf16[192,1024]{1,0:T(8,128)(2,1)S(1)} all-gather(bf16[48,1024]{1,0:T(8,128)(2,1)} %param.6), channel_id=1, replica_groups=mesh['row'=8,'col'=4] {'col'}, dimensions={0}, use_global_device_ids=true | all-gather | bytes 491520 | tf_op jit(solution)/shard_map/all_gather | solution.py:40
  39.6 0.0 slice-start.1
  39.6 5.9 %convolution_convert_fusion.3 = bf16[192,3584]{1,0:T(8,128)(2,1)} fusion(bf16[192,1024]{1,0:T(8,128)(2,1)S(1)} %all_gather.13, bf16[1024,3584]{1,0:T(8,128)(2,1)} %param.7), kind=kOutput, calls=%fused_computation.5 | convolution fusion | flops 1409974272 | bytes 9109504 | tf_op jit(solution)/shard_map/dot_general | solution.py:44
  45.5 0.0 slice-done
  45.5 0.0 slice-done.1
  45.5 3.6 %convolution_convert_fusion.5 = bf16[192,3584]{1,0:T(8,128)(2,1)} fusion(bf16[192,1024]{1,0:T(8,128)(2,1)S(1)} %all_gather.12, bf16[3584,1024]{1,0:T(8,128)(2,1)S(1)} %bitcast.20), kind=kOutput, calls=%fused_computation.7 | convolution fusion | flops 1409974272 | bytes 9109504 | tf_op jit(solution)/shard_map/dot_general | solution.py:22
  49.1 0.0 all-reduce.3.cloned.1.call-update
  49.1 0.0 all-gather.3.cloned.1.call-start
  49.2 5.8 %convolution_convert_fusion.4 = bf16[192,3584]{1,0:T(8,128)(2,1)} fusion(bf16[192,1024]{1,0:T(8,128)(2,1)S(1)} %all_gather.13, bf16[1024,3584]{1,0:T(8,128)(2,1)} %param.8), kind=kOutput, calls=%fused_computation.6 | convolution fusion | flops 1409974272 | bytes 9109504 | tf_op jit(solution)/shard_map/dot_general | solution.py:48
  55.0 0.0 all-gather.3.cloned.1.call-update
  55.0 0.0 reduce-scatter.2.cloned.1.call-start
  55.0 60.9 %all-reduce.3.cloned.1.call-done = (bf16[192,3584]{1,0:T(8,128)(2,1)}, bf16[192,3584]{1,0:T(8,128)(2,1)}) async-done(((bf16[192,3584]{1,0:T(8,128)(2,1)}, bf16[192,3584]{1,0:T(8,128)(2,1)}), (bf16[192,3584]{1,0:T(8,128)(2,1)}, bf16[192,3584]{1,0:T(8,128)(2,1)})) %all-reduce.3.cloned.1.call-update) | async-done | bytes 2752528 | tf_op jit(solution)/shard_map/psum | solution.py:50
  116.0 7.0 %fusion.1 = bf16[1024,3584]{0,1:T(8,128)(2,1)} fusion(bf16[192,1024]{1,0:T(8,128)(2,1)S(1)} %all_gather.13, bf16[192,3584]{1,0:T(8,128)(2,1)} %get-tuple-element.9, bf16[192,3584]{1,0:T(8,128)(2,1)} %get-tuple-element.8), kind=kOutput, calls=%fused_computation.4 | convolution fusion | flops 1418461184 | bytes 10485760 | tf_op jit(solution)/shard_map/dot_general | solution.py:16
  123.0 10.2 %copy.10 = bf16[1024,3584]{1,0:T(8,128)(2,1)} copy(bf16[1024,3584]{0,1:T(8,128)(2,1)} %fusion.1) | data formatting | bytes 14680064
  133.2 50.4 %all-gather.3.cloned.1.call-done = bf16[1536,3584]{1,0:T(8,128)(2,1)} async-done(((bf16[192,3584]{1,0:T(8,128)(2,1)}), bf16[1536,3584]{1,0:T(8,128)(2,1)}) %all-gather.3.cloned.1.call-update) | async-done | bytes 11010064 | tf_op jit(solution)/shard_map/all_gather | solution.py:9
  183.6 6.4 %reduce_sum.12 = bf16[192,3584]{1,0:T(8,128)(2,1)S(1)} reduce(bf16[8,192,3584]{2,1,0:T(8,128)(2,1)} %bitcast.18, bf16[]{:T(256)} %constant.1.clone.1), dimensions={0}, to_apply=%region_1.0 | reduce | flops 4816896 | bytes 12386306 | tf_op jit(solution)/shard_map/reduce_sum | solution.py:9
  190.0 3.0 %fusion.4 = bf16[192,3584]{1,0:T(8,128)(2,1)S(1)} fusion(bf16[192,3584]{1,0:T(8,128)(2,1)S(1)} %reduce_sum.12, bf16[192,3584]{1,0:T(8,128)(2,1)} %get-tuple-element.8, bf16[192,3584]{1,0:T(8,128)(2,1)} %get-tuple-element.9), kind=kLoop, calls=%fused_computation.16 | loop fusion | flops 8945664 | bytes 5505024 | tf_op jit(solution)/shard_map/convert_element_type | solution.py:33
  192.9 0.0 copy-start
  193.0 0.0 copy-start.2
  193.0 5.7 %fusion.18 = f32[192,1024]{1,0:T(8,128)S(1)} fusion(bf16[192,3584]{1,0:T(8,128)(2,1)S(1)} %fusion.4, bf16[1024,3584]{1,0:T(8,128)(2,1)} %param.7), kind=kOutput, calls=%fused_computation.28 | convolution fusion | flops 1409286144 | bytes 9502720 | tf_op jit(solution)/shard_map/dot_general | solution.py:22
  198.7 0.0 copy-done
  198.7 0.0 copy-done.2
  198.7 6.4 %fusion.14 = bf16[192,1024]{1,0:T(8,128)(2,1)} fusion(f32[192,1024]{1,0:T(8,128)S(1)} %fusion.18, bf16[1024,3584]{1,0:T(8,128)(2,1)} %param.8, bf16[192,3584]{1,0:T(8,128)(2,1)S(1)} %copy-done, bf16[192,3584]{1,0:T(8,128)(2,1)S(1)} %copy-done.2), kind=kOutput, calls=%fused_computation.26 | convolution fusion | flops 1415184384 | bytes 11272192 | tf_op jit(solution)/shard_map/dot_general | solution.py:22
  205.2 0.0 reduce-scatter.2.cloned.1.call-update
  205.2 5.2 %fusion = bf16[1024,3584]{0,1:T(8,128)(2,1)} fusion(bf16[192,3584]{1,0:T(8,128)(2,1)S(1)} %fusion.4, bf16[192,1024]{1,0:T(8,128)(2,1)S(1)} %all_gather.13), kind=kOutput, calls=%fused_computation.3 | convolution fusion | flops 1412956160 | bytes 9109504 | tf_op jit(solution)/shard_map/dot_general | solution.py:16
  210.4 0.0 copy-start.1
  210.4 10.1 %copy.9 = bf16[1024,3584]{1,0:T(8,128)(2,1)} copy(bf16[1024,3584]{0,1:T(8,128)(2,1)} %fusion) | data formatting | bytes 14680064
  220.5 0.0 copy-done.1
  220.5 5.3 %convolution_convert_fusion = bf16[3584,1024]{1,0:T(8,128)(2,1)} fusion(bf16[192,1024]{1,0:T(8,128)(2,1)S(1)} %all_gather.12, bf16[192,3584]{1,0:T(8,128)(2,1)S(1)} %reduce_sum.12, bf16[192,3584]{1,0:T(8,128)(2,1)S(1)} %copy-done.1), kind=kOutput, calls=%fused_computation | convolution fusion | flops 1418461184 | bytes 10485760 | tf_op jit(solution)/shard_map/dot_general | solution.py:16
  225.7 0.4 reduce-scatter.2.cloned.1.call-done
  (1 shorter events, 0.0 us)
Async XLA Ops:
  7.2 108.8 %all-reduce.3.cloned.1.call-start = ((), (), s32[]{:S(2)}) async-start(), calls=%async_computation.3 | async-start | bytes 5505024 | tf_op jit(solution)/shard_map/psum | solution.py:50
  23.7 21.8 %slice-start = ((s8[7340032]{0:T(1024)(128)(4,1)}), s8[4194304]{0:T(1024)(128)(4,1)S(1)}, s32[]{:S(2)}) async-start(s8[7340032]{0:T(1024)(128)(4,1)} %bitcast.19), calls=%async_computation.4 | async-start | bytes 8388608
  39.6 5.9 %slice-start.1 = ((s8[7340032]{0:T(1024)(128)(4,1)}), s8[3145728]{0:T(1024)(128)(4,1)S(1)}, s32[]{:S(2)}) async-start(s8[7340032]{0:T(1024)(128)(4,1)} %bitcast.19), calls=%async_computation.5 | async-start | bytes 6291456
  49.1 134.4 %all-gather.3.cloned.1.call-start = ((), (), s32[]{:S(2)}) async-start(), calls=%async_computation.2 | async-start | bytes 12386304 | tf_op jit(solution)/shard_map/all_gather | solution.py:9
  55.0 171.2 %reduce-scatter.2.cloned.1.call-start = ((), (), s32[]{:S(2)}) async-start(), calls=%async_computation.1 | async-start | bytes 491520 | tf_op jit(solution)/shard_map/reduce_scatter | solution.py:59
  192.9 5.8 %copy-start = (bf16[192,3584]{1,0:T(8,128)(2,1)S(1)}, bf16[192,3584]{1,0:T(8,128)(2,1)}, u32[]{:S(2)}) copy-start(bf16[192,3584]{1,0:T(8,128)(2,1)} %get-tuple-element.9) | copy-start | bytes 4128772
  193.0 5.8 %copy-start.2 = (bf16[192,3584]{1,0:T(8,128)(2,1)S(1)}, bf16[192,3584]{1,0:T(8,128)(2,1)}, u32[]{:S(2)}) copy-start(bf16[192,3584]{1,0:T(8,128)(2,1)} %get-tuple-element.8) | copy-start | bytes 4128772
  210.4 10.1 %copy-start.1 = (bf16[192,3584]{1,0:T(8,128)(2,1)S(1)}, bf16[192,3584]{1,0:T(8,128)(2,1)}, u32[]{:S(2)}) copy-start(bf16[192,3584]{1,0:T(8,128)(2,1)} %get-tuple-element.9) | copy-start | bytes 4128772
Sparse Core Ops, SparseCore 0:
  49.3 66.6 all-reduce.2
  118.4 65.0 all-gather.2
  205.3 20.8 reduce-scatter.1
